TPU v7x, 512 devices: a whole 4x4x16 slice. The times are simulated.
512 devices in a mesh: dp: 64 (over z, x_lo, core), slab: 8 (over y, x_hi).
Axes of the slice: x: 4 (x_hi: 2, x_lo: 2; x = x_hi * 2 + x_lo), y: 4, z: 16, core: 2. Of those that a mesh axis runs over, the one named last changes fastest.
Arguments:
- voxels: bfloat16 [64, 8, 12, 32, 128], P('dp', None, None, 'slab'), may hold values from -16 to 16
- occupancy: int32 [64, 8, 12, 32], P('dp', None, None, 'slab'), may hold values 0 or 1
- out_grad: bfloat16 [64, 8, 12, 32, 128], P('dp', None, None, 'slab'), may hold values from -192 to 192
- weights: bfloat16 [2, 3456, 128], replicated, may hold values from -5 to 5
- master: float32 [2, 3456, 128], P(None, 'dp', 'slab'), may hold values from -5 to 5
- moment: float32 [2, 3456, 128], P(None, 'dp', 'slab'), may hold values from -18 to 18
- second: float32 [2, 3456, 128], P(None, 'dp', 'slab'), may hold values from 1 to 10
- teacher: float32 [2, 3456, 128], P(None, 'dp', 'slab'), may hold values from -5 to 5
Outputs:
- new_master: float32 [2, 3456, 128], P(None, 'dp', 'slab')
- new_moment: float32 [2, 3456, 128], P(None, 'dp', 'slab')
- new_second: float32 [2, 3456, 128], P(None, 'dp', 'slab')
- new_teacher: float32 [2, 3456, 128], P(None, 'dp', 'slab')
- new_weights: bfloat16 [2, 3456, 128], P(None, None, 'slab')
All inputs are finite; a program needn't handle non-finite values. No bound on the sum of `occupancy` on one device may be relied on, other than what follows from the above.
Results may differ from a plain program's by a relative error of at most 0.0013.
Values may be sent and summed in bfloat16 or wider, within the bound.
No kernel may reach another device: no remote copies, remote signals or barrier semaphores. Data moves between devices by JAX's collectives and lax.ppermute only.
A program may use at most 64 MiB of HBM per device.

v0:
```python
import jax
import jax.numpy as jnp
from jax import lax
from jax.sharding import PartitionSpec as P

C = 128
TAPS = 27
STEP_COUNT = 10


beta_first = 0.9
beta_second = 0.999
learning_rate = 0.01
weight_decay = 0.05
teacher_keep = 0.99
adam_epsilon = 1e-08


def with_halo(cells, sides, width):
    for axis, dim in sides:
        count = lax.axis_size(axis)
        ends = count - 1
        head = lax.slice_in_dim(cells, 0, width, axis=dim)
        tail = lax.slice_in_dim(cells, cells.shape[dim] - width, cells.shape[dim], axis=dim)
        cells = jnp.concatenate(
            [
                lax.ppermute(tail, axis, [(i, (i + 1) % count) for i in range(ends)]),
                cells,
                lax.ppermute(head, axis, [((i + 1) % count, i) for i in range(ends)]),
            ],
            axis=dim,
        )
    return cells


def tap_corners():
    return [
        (along_x, along_y, along_z)
        for along_x in range(3)
        for along_y in range(3)
        for along_z in range(3)
    ]


def unit_scale():
    return (TAPS * C) ** (-0.5)


def silu_slope(values):
    logistic = jax.nn.sigmoid(values)
    return logistic * (1.0 + values * (1.0 - logistic))


def take_window(padded, start, extent):
    window = padded[
        start[0] : start[0] + extent[0],
        start[1] : start[1] + extent[1],
        start[2] : start[2] + extent[2],
    ]
    return window.reshape(-1, window.shape[-1])


def forward_conv(padded, weight_rows, extent):
    channels = weight_rows.shape[1]
    summed = jnp.zeros((extent[0] * extent[1] * extent[2], channels), jnp.float32)
    for tap_index, corner in enumerate(tap_corners()):
        window = take_window(padded, corner, extent)
        block = weight_rows[tap_index * channels : (tap_index + 1) * channels]
        summed = summed + jnp.dot(window, block, preferred_element_type=jnp.float32)
    return (summed * unit_scale()).reshape(extent + (channels,))


def transposed_conv(padded_grad, weight_rows, extent):
    channels = weight_rows.shape[1]
    summed = jnp.zeros((extent[0] * extent[1] * extent[2], channels), jnp.float32)
    for tap_index, corner in enumerate(tap_corners()):
        start = (2 - corner[0], 2 - corner[1], 2 - corner[2])
        window = take_window(padded_grad, start, extent)
        block = weight_rows[tap_index * channels : (tap_index + 1) * channels]
        summed = summed + lax.dot_general(
            window, block, (((1,), (1,)), ((), ())), preferred_element_type=jnp.float32
        )
    return (summed * unit_scale()).reshape(extent + (channels,))


def weight_grad(padded, grad_field, extent):
    grad_rows = grad_field.reshape(-1, grad_field.shape[-1])
    blocks = []
    for corner in tap_corners():
        window = take_window(padded, corner, extent)
        blocks.append(
            lax.dot_general(
                window, grad_rows, (((0,), (0,)), ((), ())), preferred_element_type=jnp.float32
            )
        )
    return jnp.concatenate(blocks, axis=0) * unit_scale()


def adam_update(master, moment, second, teacher, gradient):
    new_moment = beta_first * moment + (1.0 - beta_first) * gradient
    new_second = beta_second * second + (1.0 - beta_second) * gradient * gradient
    first_fix = 1.0 - beta_first**STEP_COUNT
    second_fix = 1.0 - beta_second**STEP_COUNT
    ratio = new_moment / first_fix / (jnp.sqrt(new_second / second_fix) + adam_epsilon)
    new_master = master - learning_rate * (ratio + weight_decay * master)
    new_teacher = teacher_keep * teacher + (1.0 - teacher_keep) * new_master
    return (new_master, new_moment, new_second, new_teacher)


def local(voxels, occupancy, out_grad, weights, master, moment, second, teacher):
    own_cells = voxels[0]
    extent = tuple(own_cells.shape[:3])
    occupied = occupancy[0].astype(jnp.float32)[..., None]
    plane_pad = ((1, 1), (1, 1), (0, 0), (0, 0))
    rim_input = with_halo(own_cells, (("slab", 2),), 1)
    padded_in = jnp.pad(rim_input, plane_pad)
    pre_one = forward_conv(padded_in, weights[0], extent)
    act_one = (occupied * jax.nn.silu(pre_one)).astype(jnp.bfloat16)
    rim_hidden = with_halo(act_one, (("slab", 2),), 1)
    padded_act = jnp.pad(rim_hidden, plane_pad)
    pre_two = forward_conv(padded_act, weights[1], extent)
    grad_two = (out_grad[0].astype(jnp.float32) * occupied * silu_slope(pre_two)).astype(
        jnp.bfloat16
    )
    rim_grad = with_halo(grad_two, (("slab", 2),), 1)
    padded_grad = jnp.pad(rim_grad, plane_pad)
    wgrad_two = weight_grad(padded_act, grad_two, extent)
    back_one = transposed_conv(padded_grad, weights[1], extent)
    grad_one = (back_one * occupied * silu_slope(pre_one)).astype(jnp.bfloat16)
    wgrad_one = weight_grad(padded_in, grad_one, extent)
    weight_grads = jnp.stack([wgrad_one, wgrad_two])
    row_sums = lax.psum_scatter(weight_grads, "dp", scatter_dimension=1, tiled=True)
    gradient = lax.psum_scatter(row_sums, "slab", scatter_dimension=2, tiled=True)
    new_master, new_moment, new_second, new_teacher = adam_update(
        master, moment, second, teacher, gradient
    )
    fresh_weights = new_master.astype(jnp.bfloat16)
    new_weights = lax.all_gather(fresh_weights, "dp", axis=1, tiled=True)
    return (new_master, new_moment, new_second, new_teacher, new_weights)


def solution(mesh):
    in_specs = (
        P("dp", None, None, "slab", None),
        P("dp", None, None, "slab"),
        P("dp", None, None, "slab", None),
        P(),
        P(None, "dp", "slab"),
        P(None, "dp", "slab"),
        P(None, "dp", "slab"),
        P(None, "dp", "slab"),
    )
    out_specs = (
        P(None, "dp", "slab"),
        P(None, "dp", "slab"),
        P(None, "dp", "slab"),
        P(None, "dp", "slab"),
        P(None, None, "slab"),
    )
    return jax.shard_map(local, mesh=mesh, in_specs=in_specs, out_specs=out_specs, check_vma=False)
```

profile of v0, /device:TPU:1, one launch (start us, length us, event | category | flops | bytes accessed | tf_op | source)
XLA Modules:
  0.0 662.1 jit_solution(6944818351448994479)
XLA Ops:
  7.2 0.9 copy.675
  8.1 5.5 collective-permute-start
  13.6 1.3 collective-permute-start.1
  14.9 0.9 copy_convert_fusion
  15.9 0.7 fusion.352
  16.9 2.9 collective-permute-done.1
  20.0 0.6 fusion.347
  21.9 0.8 copy-done
  27.4 4.0 collective-permute-start.2
  31.4 1.3 collective-permute-start.3
  32.8 4.7 collective-permute-done.3
  37.7 0.3 fusion.345
  44.3 4.6 collective-permute-start.4
  48.9 1.5 collective-permute-start.5
  52.2 0.2 fusion.21
  52.5 0.2 fusion.20
  53.2 0.3 fusion.18
  53.9 0.2 fusion.16
  54.4 0.2 fusion.14
  54.6 0.2 fusion.13
  54.9 0.2 fusion.12
  55.1 0.2 fusion.11
  55.3 0.2 fusion.10
  55.6 0.2 fusion.9
  56.0 0.2 fusion.7
  56.9 0.3 fusion.343
  60.9 0.2 convolution_add_fusion.13
  63.9 0.2 fusion.54
  64.2 0.2 fusion.53
  64.4 0.2 fusion.52
  64.6 0.2 fusion.51
  64.9 0.2 fusion.50
  65.1 0.2 fusion.49
  65.4 0.2 fusion.48
  65.6 0.2 fusion.47
  65.8 0.2 fusion.46
  66.1 0.2 fusion.45
  66.3 0.2 fusion.44
  66.5 0.2 fusion.5
  66.8 0.2 fusion.43
  67.0 0.2 fusion.4
  67.3 0.2 fusion.42
  67.5 0.2 fusion.41
  67.7 0.2 fusion.40
  68.0 0.2 fusion.39
  68.2 0.2 fusion.38
  68.5 0.2 fusion.37
  68.7 0.2 fusion.36
  68.9 0.2 fusion.35
  69.2 0.2 fusion.34
  69.4 0.2 fusion.33
  69.6 0.2 fusion.32
  69.9 0.2 fusion.31
  70.3 0.2 pad_maximum_fusion
  70.5 14.0 %copy.534 = f32[2,3456,128]{2,0,1:T(2,128)} copy(f32[2,3456,128]{2,1,0:T(8,128)S(1)} %pad_maximum_fusion) | data formatting | bytes 7077888 | tf_op jit(solution)/shard_map/stack | solution.py:131
  84.5 1.3 dynamic-slice
  85.8 1.3 dynamic-slice.2
  88.4 449.9 %all-reduce.7.cloned.1.call-done = f32[2,3456,128]{2,0,1:T(2,128)} async-done(((f32[2,3456,128]{2,0,1:T(2,128)}), f32[2,3456,128]{2,0,1:T(2,128)}) %all-reduce.7.cloned.1.call-update) | async-done | bytes 3538960
  538.3 0.8 constant_dynamic-slice_fusion.1
  539.2 36.3 %all-reduce.4 = f32[2,54,128]{1,0,2:T(2,128)S(1)} all-reduce(f32[2,54,128]{1,0,2:T(2,128)S(1)} %copy.535), channel_id=3, replica_groups=mesh['dp'=64,'slab'=8] {'slab'}, use_global_device_ids=true, to_apply=%region_1.2.clone | all-reduce | flops 13824 | bytes 110592
  575.6 0.6 fusion.341
  576.4 75.2 %all_gather.3 = bf16[2,3456,16]{2,0,1:T(2,128)(2,1)S(1)} all-gather(bf16[2,54,16]{2,0,1:T(2,128)(2,1)S(1)} %copy.539), channel_id=1, replica_groups=mesh['dp'=64,'slab'=8] {'dp'}, dimensions={1}, use_global_device_ids=true | all-gather | bytes 224640 | tf_op jit(solution)/shard_map/all_gather | solution.py:138
  651.6 3.0 copy.540
  654.6 0.6 multiply_add_fusion
  (221 shorter events, 22.8 us)
Async XLA Ops:
  7.2 531.1 %all-reduce.7.cloned.1.call-start = ((), (), s32[]{:S(2)}) async-start(), calls=%async_computation | async-start | bytes 7077888
  8.1 8.8 %collective-permute-start = (bf16[8,12,1,128]{3,1,2,0:T(8,128)(2,1)S(1)}, bf16[8,12,1,128]{3,1,2,0:T(8,128)(2,1)S(1)}, u32[]{:S(2)}, u32[]{:S(2)}) collective-permute-start(bf16[8,12,1,128]{3,1,2,0:T(8,128)(2,1)S(1)} %get-tuple-element.110), channel_id=1, source_target_pairs={{0,1},{1,2},{2,3},{3,4},{4,5},{5,6},{6,7},{8,9},{9,10},{10,11},{11... | collective-permute-start | bytes 73736 | tf_op jit(solution)/shard_map/ppermute | solution.py:27
  13.6 6.2 collective-permute-start.1
  21.1 1.5 copy-start
  23.6 1.2 copy-start.1
  27.4 5.4 collective-permute-start.2
  31.4 6.1 collective-permute-start.3
  42.7 1.2 copy-start.2
  44.3 12.4 %collective-permute-start.4 = (bf16[8,12,1,128]{3,0,2,1:T(8,128)(2,1)S(1)}, bf16[8,12,1,128]{3,0,2,1:T(8,128)(2,1)S(1)}, u32[]{:S(2)}, u32[]{:S(2)}) collective-permute-start(bf16[8,12,1,128]{3,0,2,1:T(8,128)(2,1)S(1)} %get-tuple-element.114), channel_id=1, source_target_pairs={{0,1},{1,2},{2,3},{3,4},{4,5},{5,6},{6,7},{8,9},{9,10},{10,11},{11... | collective-permute-start | bytes 73736 | tf_op jit(solution)/shard_map/ppermute | solution.py:27
  48.9 7.7 %collective-permute-start.5 = (bf16[8,12,1,128]{3,0,2,1:T(8,128)(2,1)S(1)}, bf16[8,12,1,128]{3,0,2,1:T(8,128)(2,1)S(1)}, u32[]{:S(2)}, u32[]{:S(2)}) collective-permute-start(bf16[8,12,1,128]{3,0,2,1:T(8,128)(2,1)S(1)} %get-tuple-element.115), channel_id=1, source_target_pairs={{1,0},{2,1},{3,2},{4,3},{5,4},{6,5},{7,6},{9,8},{10,9},{11,10},{12... | collective-permute-start | bytes 73736 | tf_op jit(solution)/shard_map/ppermute | solution.py:29
  84.5 491.1 %copy-start.4 = (f32[2,54,16]{1,2,0:T(8,128)S(1)}, f32[2,54,16]{1,2,0:T(8,128)}, u32[]{:S(2)}) copy-start(f32[2,54,16]{1,2,0:T(8,128)} %param.12) | copy-start | bytes 20740
  84.5 491.1 %copy-start.5 = (f32[2,54,16]{1,2,0:T(8,128)S(1)}, f32[2,54,16]{1,2,0:T(8,128)}, u32[]{:S(2)}) copy-start(f32[2,54,16]{1,2,0:T(8,128)} %param.13) | copy-start | bytes 20740
  84.5 491.1 %copy-start.6 = (f32[2,54,16]{1,2,0:T(8,128)S(1)}, f32[2,54,16]{1,2,0:T(8,128)}, u32[]{:S(2)}) copy-start(f32[2,54,16]{1,2,0:T(8,128)} %param.14) | copy-start | bytes 20740
  576.2 78.3 %copy-start.3 = (f32[2,54,16]{1,2,0:T(8,128)}, f32[2,54,16]{1,2,0:T(8,128)S(1)}, u32[]{:S(2)}) copy-start(f32[2,54,16]{1,2,0:T(8,128)S(1)} %get-tuple-element.31) | copy-start | bytes 20740
  576.4 78.2 %copy-start.7 = (f32[2,54,16]{1,2,0:T(8,128)S(1)}, f32[2,54,16]{1,2,0:T(8,128)}, u32[]{:S(2)}) copy-start(f32[2,54,16]{1,2,0:T(8,128)} %param.15) | copy-start | bytes 20740
Sparse Core Ops, SparseCore 0:
  84.6 453.6 all-reduce.6
where the time goes:
time: 663 us; the launch traced here: 662 us
  waiting for transfers between devices  458 us (69%)
  blocking collectives  112 us (17%)
  local copies, waits for them, and re-layouts  27.2 us (4%)
  matrix products  26.2 us (4%)
  starting transfers between devices  18.3 us (3%)
  between operations  16.9 us (3%)
    unnamed x2, waiting for transfers between devices  450 us
    all_gather x1, blocking collectives, local(): new_weights = lax.all_gather(fresh_weights, 'dp', axis=1, tiled=True)  75.2 us
    unnamed x1, blocking collectives  36.3 us
    ppermute x3, starting transfers between devices, with_halo(): lax.ppermute(tail, axis, [(i, (i + 1) % count) for i in range(ends)])  14.2 us
    another operation x1, local copies, waits for them, and re-layouts, local(): weight_grads = jnp.stack([wgrad_one, wgrad_two])  14 us
  transfers between devices with their start and end apart: 7, of which 3 were waited for; matrix products, arithmetic and copies ran while one was open for 2% of the time, Pallas kernels for 0%

commit v1 on v0

--- a/solution.py
+++ b/solution.py
@@ -112,49 +112,82 @@
     extent = tuple(own_cells.shape[:3])
     occupied = occupancy[0].astype(jnp.float32)[..., None]
     plane_pad = ((1, 1), (1, 1), (0, 0), (0, 0))
-    rim_input = with_halo(own_cells, (("slab", 2),), 1)
+    rim_input = with_halo(own_cells, ((COLUMN_AXES, 2),), 1)
     padded_in = jnp.pad(rim_input, plane_pad)
     pre_one = forward_conv(padded_in, weights[0], extent)
     act_one = (occupied * jax.nn.silu(pre_one)).astype(jnp.bfloat16)
-    rim_hidden = with_halo(act_one, (("slab", 2),), 1)
+    rim_hidden = with_halo(act_one, ((COLUMN_AXES, 2),), 1)
     padded_act = jnp.pad(rim_hidden, plane_pad)
     pre_two = forward_conv(padded_act, weights[1], extent)
     grad_two = (out_grad[0].astype(jnp.float32) * occupied * silu_slope(pre_two)).astype(
         jnp.bfloat16
     )
-    rim_grad = with_halo(grad_two, (("slab", 2),), 1)
+    rim_grad = with_halo(grad_two, ((COLUMN_AXES, 2),), 1)
     padded_grad = jnp.pad(rim_grad, plane_pad)
     wgrad_two = weight_grad(padded_act, grad_two, extent)
     back_one = transposed_conv(padded_grad, weights[1], extent)
     grad_one = (back_one * occupied * silu_slope(pre_one)).astype(jnp.bfloat16)
     wgrad_one = weight_grad(padded_in, grad_one, extent)
     weight_grads = jnp.stack([wgrad_one, wgrad_two])
-    row_sums = lax.psum_scatter(weight_grads, "dp", scatter_dimension=1, tiled=True)
-    gradient = lax.psum_scatter(row_sums, "slab", scatter_dimension=2, tiled=True)
+    gradient = scatter_rows_and_columns(weight_grads, master.shape)
     new_master, new_moment, new_second, new_teacher = adam_update(
         master, moment, second, teacher, gradient
     )
     fresh_weights = new_master.astype(jnp.bfloat16)
-    new_weights = lax.all_gather(fresh_weights, "dp", axis=1, tiled=True)
+    new_weights = gather_rows(fresh_weights)
     return (new_master, new_moment, new_second, new_teacher, new_weights)
 
 
+ROW_AXES = ("z", "x_lo", "core")
+COLUMN_AXES = ("y", "x_hi")
+
+
+def scatter_rows_and_columns(weight_grads, own_shape):
+    layers, rows, cols = own_shape
+    z, x_lo, core = (lax.axis_size(name) for name in ROW_AXES)
+    y, x_hi = (lax.axis_size(name) for name in COLUMN_AXES)
+    blocks = weight_grads.reshape(layers, z, x_lo, core, rows, y, x_hi, cols)
+    blocks = blocks.transpose(3, 5, 6, 2, 1, 0, 4, 7)
+    blocks = lax.psum_scatter(blocks, "core", scatter_dimension=0, tiled=True)[0]
+    blocks = lax.psum_scatter(blocks, "y", scatter_dimension=0, tiled=True)[0]
+    blocks = blocks.reshape((x_hi * x_lo,) + blocks.shape[2:])
+    blocks = lax.psum_scatter(blocks, ("x_hi", "x_lo"), scatter_dimension=0, tiled=True)[0]
+    blocks = lax.psum_scatter(blocks, "z", scatter_dimension=0, tiled=True)[0]
+    return blocks
+
+
+def gather_rows(fresh_weights):
+    layers, rows, cols = fresh_weights.shape
+    gathered = lax.all_gather(fresh_weights, "z", axis=0)
+    gathered = lax.all_gather(gathered, ("x_lo", "core"), axis=0)
+    gathered = gathered.reshape((-1,) + gathered.shape[1:])
+    x_lo, core = lax.axis_size("x_lo"), lax.axis_size("core")
+    gathered = gathered.reshape((x_lo, core) + gathered.shape[1:])
+    gathered = gathered.transpose(3, 2, 0, 1, 4, 5)
+    return gathered.reshape(layers, -1, cols)
+
+
 def solution(mesh):
+    rows_over, columns_over = mesh.shape["dp"], mesh.shape["slab"]
+    fine = jax.sharding.Mesh(
+        mesh.devices.reshape(rows_over // 4, 2, 2, columns_over // 2, 2), ROW_AXES + COLUMN_AXES
+    )
+    dp, slab = ROW_AXES, COLUMN_AXES
     in_specs = (
-        P("dp", None, None, "slab", None),
-        P("dp", None, None, "slab"),
-        P("dp", None, None, "slab", None),
+        P(dp, None, None, slab, None),
+        P(dp, None, None, slab),
+        P(dp, None, None, slab, None),
         P(),
-        P(None, "dp", "slab"),
-        P(None, "dp", "slab"),
-        P(None, "dp", "slab"),
-        P(None, "dp", "slab"),
+        P(None, dp, slab),
+        P(None, dp, slab),
+        P(None, dp, slab),
+        P(None, dp, slab),
     )
     out_specs = (
-        P(None, "dp", "slab"),
-        P(None, "dp", "slab"),
-        P(None, "dp", "slab"),
-        P(None, "dp", "slab"),
-        P(None, None, "slab"),
+        P(None, dp, slab),
+        P(None, dp, slab),
+        P(None, dp, slab),
+        P(None, dp, slab),
+        P(None, None, slab),
     )
-    return jax.shard_map(local, mesh=mesh, in_specs=in_specs, out_specs=out_specs, check_vma=False)
+    return jax.shard_map(local, mesh=fine, in_specs=in_specs, out_specs=out_specs, check_vma=False)

time: 663 us -> 355 us (0.54)
  waiting for transfers between devices: 458 us -> 196 us
  blocking collectives: 112 us -> 47.1 us
  local copies, waits for them, and re-layouts: 27.2 us -> 40.6 us
    unnamed x2 -> x4, waiting for transfers between devices: 450 us -> 0.07 us
    reduce_scatter x0 -> x4, waiting for transfers between devices: none -> 189 us  [the longest x1 61.4 us: scatter_rows_and_columns(): blocks = lax.psum_scatter(blocks, 'z', scatter_dimension=0, tiled=True)[0]]
    unnamed x1 -> x0, blocking collectives: 36.3 us -> none
    all_gather x1 -> x2, blocking collectives: 75.2 us -> 47.1 us  [the longest x1 26.1 us: gather_rows(): gathered = lax.all_gather(gathered, ('x_lo', 'core'), axis=0)]
    mul x0 -> x4, local copies, waits for them, and re-layouts: none -> 23.2 us  [weight_grad(): return jnp.concatenate(blocks, axis=0) * unit_scale()]
    another operation x1 -> x0, local copies, waits for them, and re-layouts: 14 us -> none  [local(): weight_grads = jnp.stack([wgrad_one, wgrad_two])]
    transpose x0 -> x2, local copies, waits for them, and re-layouts: none -> 8.67 us  [the longest x1 8.13 us: scatter_rows_and_columns(): blocks = blocks.transpose(3, 5, 6, 2, 1, 0, 4, 7)]
  transfers between devices with their start and end apart: 7 -> 10, of which waited for: 3 -> 6; matrix products, arithmetic and copies ran while one was open for 2% -> 6% of each run, Pallas kernels for 0% -> 0%
where the time goes in v1:
time: 355 us
  waiting for transfers between devices  196 us (55%)
  blocking collectives  47.1 us (13%)
  local copies, waits for them, and re-layouts  40.6 us (11%)
  matrix products  26.3 us (7%)
  starting transfers between devices  18.2 us (5%)
  between operations  15.3 us (4%)
  other arithmetic  10.9 us (3%)
    reduce_scatter x1, waiting for transfers between devices, scatter_rows_and_columns(): blocks = lax.psum_scatter(blocks, 'z', scatter_dimension=0, tiled=True)[0]  61.4 us
    reduce_scatter x1, waiting for transfers between devices, scatter_rows_and_columns(): blocks = lax.psum_scatter(blocks, 'y', scatter_dimension=0, tiled=True)[0]  57.7 us
    reduce_scatter x1, waiting for transfers between devices, scatter_rows_and_columns(): lax.psum_scatter(blocks, 'core', scatter_dimension=0, tiled=True)[0]  37.2 us
    reduce_scatter x1, waiting for transfers between devices, scatter_rows_and_columns(): lax.psum_scatter(blocks, ('x_hi', 'x_lo'), scatter_dimension=0, tiled=True)  32.3 us
    all_gather x1, blocking collectives, gather_rows(): gathered = lax.all_gather(gathered, ('x_lo', 'core'), axis=0)  26.1 us
    mul x4, local copies, waits for them, and re-layouts, weight_grad(): return jnp.concatenate(blocks, axis=0) * unit_scale()  23.2 us
    all_gather x1, blocking collectives, gather_rows(): gathered = lax.all_gather(fresh_weights, 'z', axis=0)  21 us
    ppermute x3, starting transfers between devices, with_halo(): lax.ppermute(tail, axis, [(i, (i + 1) % count) for i in range(ends)])  14.2 us
  transfers between devices with their start and end apart: 10, of which 6 were waited for; matrix products, arithmetic and copies ran while one was open for 6% of the time, Pallas kernels for 0%

profile of v1, /device:TPU:1, one launch (start us, length us, event | category | flops | bytes accessed | tf_op | source)
XLA Modules:
  0.0 354.6 jit_solution(17328011585009046061)
XLA Ops:
  7.2 0.9 copy.735
  8.1 5.5 %collective-permute-start = (bf16[8,12,1,128]{3,1,2,0:T(8,128)(2,1)S(1)}, bf16[8,12,1,128]{3,1,2,0:T(8,128)(2,1)S(1)}, u32[]{:S(2)}, u32[]{:S(2)}) collective-permute-start(bf16[8,12,1,128]{3,1,2,0:T(8,128)(2,1)S(1)} %get-tuple-element.85), channel_id=1, source_target_pairs={{0,1},{1,2},{2,3},{3,4},{4,5},{5,6},{6,7},{8,9},{9,10},{10,11},{11... | collective-permute-start | bytes 73736 | tf_op jit(solution)/shard_map/ppermute | solution.py:27
  13.6 1.3 collective-permute-start.1
  14.9 0.9 copy_convert_fusion
  15.9 0.7 fusion.354
  16.9 2.9 collective-permute-done.1
  20.0 0.5 fusion.349
  21.8 0.8 copy-done
  27.3 4.0 %collective-permute-start.2 = (bf16[8,12,1,128]{3,0,2,1:T(8,128)(2,1)S(1)}, bf16[8,12,1,128]{3,0,2,1:T(8,128)(2,1)S(1)}, u32[]{:S(2)}, u32[]{:S(2)}) collective-permute-start(bf16[8,12,1,128]{3,0,2,1:T(8,128)(2,1)S(1)} %get-tuple-element.93), channel_id=1, source_target_pairs={{0,1},{1,2},{2,3},{3,4},{4,5},{5,6},{6,7},{8,9},{9,10},{10,11},{11... | collective-permute-start | bytes 73736 | tf_op jit(solution)/shard_map/ppermute | solution.py:27
  31.3 1.3 collective-permute-start.3
  32.7 4.7 %collective-permute-done.3 = bf16[8,12,1,128]{3,0,2,1:T(8,128)(2,1)S(1)} collective-permute-done((bf16[8,12,1,128]{3,0,2,1:T(8,128)(2,1)S(1)}, bf16[8,12,1,128]{3,0,2,1:T(8,128)(2,1)S(1)}, u32[]{:S(2)}, u32[]{:S(2)}) %collective-permute-start.3) | collective-permute-done | bytes 24608 | tf_op jit(solution)/shard_map/ppermute | solution.py:29
  37.6 0.3 fusion.347
  44.2 4.6 %collective-permute-start.4 = (bf16[8,12,1,128]{3,0,2,1:T(8,128)(2,1)S(1)}, bf16[8,12,1,128]{3,0,2,1:T(8,128)(2,1)S(1)}, u32[]{:S(2)}, u32[]{:S(2)}) collective-permute-start(bf16[8,12,1,128]{3,0,2,1:T(8,128)(2,1)S(1)} %get-tuple-element.89), channel_id=1, source_target_pairs={{0,1},{1,2},{2,3},{3,4},{4,5},{5,6},{6,7},{8,9},{9,10},{10,11},{11... | collective-permute-start | bytes 73736 | tf_op jit(solution)/shard_map/ppermute | solution.py:27
  48.8 1.3 collective-permute-start.5
  50.1 0.2 fusion.29
  50.4 0.2 fusion.28
  50.6 0.2 fusion.27
  50.8 0.2 fusion.26
  51.1 0.2 fusion.25
  51.3 0.2 fusion.24
  51.5 0.2 fusion.23
  51.8 0.2 fusion.22
  52.2 0.2 fusion.20
  52.9 0.3 fusion.18
  53.7 0.2 fusion.16
  54.4 0.2 fusion.13
  55.1 0.2 fusion.10
  55.8 0.2 fusion.7
  56.4 2.2 copy.602
  58.6 9.5 %mul.224 = f32[1,16,2,2,54,4,2,16]{4,3,2,1,7,6,5,0:T(2,128)} reshape(f32[1,3456,128]{1,2,0:T(8,128)} %copy.602) | data formatting | bytes 3538944 | tf_op jit(solution)/shard_map/mul | solution.py:96
  68.3 0.3 fusion.345
  69.0 0.8 copy-done.1
  73.1 0.2 convolution_add_fusion.13
  76.7 0.2 fusion.52
  76.9 0.2 fusion.51
  77.1 0.2 fusion.50
  77.4 0.2 fusion.49
  77.6 0.2 fusion.48
  77.9 0.2 fusion.47
  78.8 0.2 fusion.5
  79.3 0.2 fusion.4
  79.5 0.2 fusion.42
  79.8 0.2 fusion.41
  80.0 0.2 fusion.40
  80.9 0.2 fusion.36
  81.2 0.2 fusion.35
  81.4 0.2 fusion.34
  81.7 0.2 fusion.33
  81.9 0.2 fusion.32
  82.2 0.2 fusion.31
  82.6 2.0 copy.597
  84.6 9.6 %mul.217 = f32[1,16,2,2,54,4,2,16]{4,3,2,1,7,6,5,0:T(2,128)} reshape(f32[1,3456,128]{1,2,0:T(8,128)} %copy.597) | data formatting | bytes 3538944 | tf_op jit(solution)/shard_map/mul | solution.py:96
  94.1 6.0 %maximum_bitcast_fusion = f32[2,4,2,2,16,2,54,16]{6,0,3,4,7,2,1,5:T(2,128)S(1)} fusion(f32[1,16,2,2,54,4,2,16]{4,3,2,1,7,6,5,0:T(2,128)} %mul.224, f32[1,16,2,2,54,4,2,16]{4,3,2,1,7,6,5,0:T(2,128)} %mul.217), kind=kLoop, calls=%fused_computation | loop fusion | flops 884736 | bytes 7077888 | tf_op jit(solution)/shard_map/transpose | solution.py:150
  100.2 8.1 %copy.603 = f32[2,4,2,2,16,2,54,16]{6,7,5,4,3,2,1,0:T(8,128)} copy(f32[2,4,2,2,16,2,54,16]{6,0,3,4,7,2,1,5:T(2,128)S(1)} %maximum_bitcast_fusion) | data formatting | bytes 7077888 | tf_op jit(solution)/shard_map/transpose | solution.py:150
  108.4 37.2 %reduce-scatter.5.cloned.1.call-done = f32[1,4,2,2,16,2,54,16]{6,7,5,4,3,2,1,0:T(8,128)} async-done(((f32[2,4,2,2,16,2,54,16]{6,7,5,4,3,2,1,0:T(8,128)}), f32[1,4,2,2,16,2,54,16]{6,7,5,4,3,2,1,0:T(8,128)}) %reduce-scatter.5.cloned.1.call-update) | async-done | bytes 1769488 | tf_op jit(solution)/shard_map/reduce_scatter | solution.py:151
  145.6 57.7 %reduce-scatter.7.cloned.1.call-done = f32[1,2,2,16,2,54,16]{5,6,4,3,2,1,0:T(8,128)} async-done(((f32[4,2,2,16,2,54,16]{5,6,4,3,2,1,0:T(8,128)}), f32[1,2,2,16,2,54,16]{5,6,4,3,2,1,0:T(8,128)}) %reduce-scatter.7.cloned.1.call-update) | async-done | bytes 442384 | tf_op jit(solution)/shard_map/reduce_scatter | solution.py:152
  203.4 32.3 %reduce-scatter.9.cloned.1.call-done = f32[1,16,2,54,16]{3,4,2,1,0:T(8,128)} async-done(((f32[4,16,2,54,16]{3,4,2,1,0:T(8,128)}), f32[1,16,2,54,16]{3,4,2,1,0:T(8,128)}) %reduce-scatter.9.cloned.1.call-update) | async-done | bytes 110608 | tf_op jit(solution)/shard_map/reduce_scatter | solution.py:154
  235.7 61.4 %reduce-scatter.11.cloned.1.call-done = f32[1,2,54,16]{2,3,1,0:T(8,128)} async-done(((f32[16,2,54,16]{2,3,1,0:T(8,128)}), f32[1,2,54,16]{2,3,1,0:T(8,128)}) %reduce-scatter.11.cloned.1.call-update) | async-done | bytes 6928 | tf_op jit(solution)/shard_map/reduce_scatter | solution.py:155
  297.1 1.3 fusion.342
  298.5 21.0 %all-gather = bf16[32,54,16]{1,2,0:T(8,128)(2,1)S(1)} all-gather(bf16[2,54,16]{1,2,0:T(8,128)(2,1)S(1)} %get-tuple-element.5), channel_id=2, replica_groups=mesh['z'=16,'x_lo'=2,'core'=2,'y'=4,'x_hi'=2] {'z'}, dimensions={0}, use_global_device_ids=true | all-gather | bytes 58752 | tf_op jit(solution)/shard_map/all_gather | solution.py:161
  319.5 26.1 %all-gather.1 = bf16[64,2,54,16]{2,3,1,0:T(8,128)(2,1)S(1)} all-gather(bf16[16,2,54,16]{2,3,1,0:T(8,128)(2,1)S(1)} %bitcast.895), channel_id=3, replica_groups=mesh['z'=16,'x_lo'=2,'core'=2,'y'=4,'x_hi'=2] {'x_lo','core'}, dimensions={0}, use_global_device_ids=true | all-gather | bytes 276480 | tf_op jit(solution)/shard_map/all_gather | solution.py:162
  345.5 0.5 copy.604
  346.1 1.4 reshape.587
  347.4 0.6 multiply_add_fusion
  (231 shorter events, 24.1 us)
Async XLA Ops:
  7.2 138.4 %reduce-scatter.5.cloned.1.call-start = ((), (), s32[]{:S(2)}) async-start(), calls=%async_computation.4 | async-start | bytes 12582912 | tf_op jit(solution)/shard_map/reduce_scatter | solution.py:151
  8.1 8.8 %collective-permute-start = (bf16[8,12,1,128]{3,1,2,0:T(8,128)(2,1)S(1)}, bf16[8,12,1,128]{3,1,2,0:T(8,128)(2,1)S(1)}, u32[]{:S(2)}, u32[]{:S(2)}) collective-permute-start(bf16[8,12,1,128]{3,1,2,0:T(8,128)(2,1)S(1)} %get-tuple-element.85), channel_id=1, source_target_pairs={{0,1},{1,2},{2,3},{3,4},{4,5},{5,6},{6,7},{8,9},{9,10},{10,11},{11... | collective-permute-start | bytes 73736 | tf_op jit(solution)/shard_map/ppermute | solution.py:27
  13.6 6.2 %collective-permute-start.1 = (bf16[8,12,1,128]{3,1,2,0:T(8,128)(2,1)S(1)}, bf16[8,12,1,128]{3,1,2,0:T(8,128)(2,1)S(1)}, u32[]{:S(2)}, u32[]{:S(2)}) collective-permute-start(bf16[8,12,1,128]{3,1,2,0:T(8,128)(2,1)S(1)} %get-tuple-element.86), channel_id=1, source_target_pairs={{1,0},{2,1},{3,2},{4,3},{5,4},{6,5},{7,6},{9,8},{10,9},{11,10},{12... | collective-permute-start | bytes 73736 | tf_op jit(solution)/shard_map/ppermute | solution.py:29
  21.0 1.5 copy-start
  23.5 1.2 copy-start.2
  27.3 5.4 %collective-permute-start.2 = (bf16[8,12,1,128]{3,0,2,1:T(8,128)(2,1)S(1)}, bf16[8,12,1,128]{3,0,2,1:T(8,128)(2,1)S(1)}, u32[]{:S(2)}, u32[]{:S(2)}) collective-permute-start(bf16[8,12,1,128]{3,0,2,1:T(8,128)(2,1)S(1)} %get-tuple-element.93), channel_id=1, source_target_pairs={{0,1},{1,2},{2,3},{3,4},{4,5},{5,6},{6,7},{8,9},{9,10},{10,11},{11... | collective-permute-start | bytes 73736 | tf_op jit(solution)/shard_map/ppermute | solution.py:27
  31.3 6.1 %collective-permute-start.3 = (bf16[8,12,1,128]{3,0,2,1:T(8,128)(2,1)S(1)}, bf16[8,12,1,128]{3,0,2,1:T(8,128)(2,1)S(1)}, u32[]{:S(2)}, u32[]{:S(2)}) collective-permute-start(bf16[8,12,1,128]{3,0,2,1:T(8,128)(2,1)S(1)} %get-tuple-element.94), channel_id=1, source_target_pairs={{1,0},{2,1},{3,2},{4,3},{5,4},{6,5},{7,6},{9,8},{10,9},{11,10},{12... | collective-permute-start | bytes 73736 | tf_op jit(solution)/shard_map/ppermute | solution.py:29
  42.6 1.2 copy-start.3
  44.2 23.9 %collective-permute-start.4 = (bf16[8,12,1,128]{3,0,2,1:T(8,128)(2,1)S(1)}, bf16[8,12,1,128]{3,0,2,1:T(8,128)(2,1)S(1)}, u32[]{:S(2)}, u32[]{:S(2)}) collective-permute-start(bf16[8,12,1,128]{3,0,2,1:T(8,128)(2,1)S(1)} %get-tuple-element.89), channel_id=1, source_target_pairs={{0,1},{1,2},{2,3},{3,4},{4,5},{5,6},{6,7},{8,9},{9,10},{10,11},{11... | collective-permute-start | bytes 73736 | tf_op jit(solution)/shard_map/ppermute | solution.py:27
  48.8 19.3 %collective-permute-start.5 = (bf16[8,12,1,128]{3,0,2,1:T(8,128)(2,1)S(1)}, bf16[8,12,1,128]{3,0,2,1:T(8,128)(2,1)S(1)}, u32[]{:S(2)}, u32[]{:S(2)}) collective-permute-start(bf16[8,12,1,128]{3,0,2,1:T(8,128)(2,1)S(1)} %get-tuple-element.90), channel_id=1, source_target_pairs={{1,0},{2,1},{3,2},{4,3},{5,4},{6,5},{7,6},{9,8},{10,9},{11,10},{12... | collective-permute-start | bytes 73736 | tf_op jit(solution)/shard_map/ppermute | solution.py:29
  68.3 1.5 copy-start.1
  108.3 95.0 %reduce-scatter.7.cloned.1.call-start = ((), (), s32[]{:S(2)}) async-start(), calls=%async_computation.5 | async-start | bytes 5242880 | tf_op jit(solution)/shard_map/reduce_scatter | solution.py:152
  145.6 151.6 %copy-start.5 = (f32[2,54,16]{1,2,0:T(8,128)S(1)}, f32[2,54,16]{1,2,0:T(8,128)}, u32[]{:S(2)}) copy-start(f32[2,54,16]{1,2,0:T(8,128)} %param.12) | copy-start | bytes 20740
  145.6 151.6 %copy-start.6 = (f32[2,54,16]{1,2,0:T(8,128)S(1)}, f32[2,54,16]{1,2,0:T(8,128)}, u32[]{:S(2)}) copy-start(f32[2,54,16]{1,2,0:T(8,128)} %param.13) | copy-start | bytes 20740
  145.6 151.6 %copy-start.7 = (f32[2,54,16]{1,2,0:T(8,128)S(1)}, f32[2,54,16]{1,2,0:T(8,128)}, u32[]{:S(2)}) copy-start(f32[2,54,16]{1,2,0:T(8,128)} %param.14) | copy-start | bytes 20740
  145.6 90.1 %reduce-scatter.9.cloned.1.call-start = ((), (), s32[]{:S(2)}) async-start(), calls=%async_computation.6 | async-start | bytes 1310720 | tf_op jit(solution)/shard_map/reduce_scatter | solution.py:154
  203.3 144.1 %copy-start.8 = (f32[2,54,16]{1,2,0:T(8,128)S(1)}, f32[2,54,16]{1,2,0:T(8,128)}, u32[]{:S(2)}) copy-start(f32[2,54,16]{1,2,0:T(8,128)} %param.15) | copy-start | bytes 20740
  203.3 93.8 %reduce-scatter.11.cloned.1.call-start = ((), (), s32[]{:S(2)}) async-start(), calls=%async_computation.7 | async-start | bytes 278528 | tf_op jit(solution)/shard_map/reduce_scatter | solution.py:155
  298.5 49.6 %copy-start.4 = (f32[2,54,16]{1,2,0:T(8,128)}, f32[2,54,16]{1,2,0:T(8,128)S(1)}, u32[]{:S(2)}) copy-start(f32[2,54,16]{1,2,0:T(8,128)S(1)} %get-tuple-element.6) | copy-start | bytes 20740
Sparse Core Ops, SparseCore 0:
  108.4 37.0 reduce-scatter.4
  148.6 54.6 reduce-scatter.6
  206.1 29.5 reduce-scatter.8
  238.6 58.5 reduce-scatter.10
